TPU v7x, 512 devices: a whole 4x8x8 slice. The times are simulated.
512 devices in a mesh: grp: 4 (over x), gx: 16 (over z_hi, y), gy: 8 (over z_lo, core).
Axes of the slice: x: 4, y: 8, z: 8 (z_hi: 2, z_lo: 4; z = z_hi * 4 + z_lo), core: 2. Of those that a mesh axis runs over, the one named last changes fastest.
Arguments:
- fwd_now: float32 [3, 64, 64, 128], P(None, 'gx', 'gy'), may hold values from -6 to 6
- fwd_prev: float32 [3, 64, 64, 128], P(None, 'gx', 'gy'), may hold values from -6 to 6
- adj_now: float32 [16, 3, 64, 64, 128], P('grp', None, 'gx', 'gy'), may hold values from -6 to 6
- adj_prev: float32 [16, 3, 64, 64, 128], P('grp', None, 'gx', 'gy'), may hold values from -6 to 6
- lame_first: float32 [64, 64, 128], P('gx', 'gy'), may hold values from 0.5 to 2
- shear_mod: float32 [64, 64, 128], P('gx', 'gy'), may hold values from 0.3 to 1.2
- buoyancy: float32 [64, 64, 128], P('gx', 'gy'), may hold values from 0.5 to 1
- master_cell: int32 [1], replicated, may hold values from 0 to 524287
- master_lag: int32 [1], replicated, may hold values from 0 to 254
- master_trace: float32 [256, 3], replicated, may hold values from -96 to 96
- receiver_cell: int32 [16], P('grp'), may hold values from 0 to 524287
- receiver_lag: int32 [16], P('grp'), may hold values from 0 to 254
- receiver_trace: float32 [16, 256, 3], P('grp'), may hold values from -96 to 96
Outputs:
- adj_final: float32 [16, 3, 64, 64, 128], P('grp', None, 'gx', 'gy')
- kernels: float32 [2, 64, 64, 128], P(None, 'gx', 'gy', 'grp')
Inputs may be any that keep to these rules, and one draw needn't show every extreme that they name: `receiver_cell`: cell index in the whole grid, numbered (x * 64 + y) * 128 + z. `master_cell`: cell index in the whole grid, numbered (x * 64 + y) * 128 + z.
All inputs are finite; a program needn't handle non-finite values.
Results may differ from a plain program's by a relative error of at most 0.00011.
Values sent between devices are 32-bit elements; how exact they have to be, the bound alone decides.
No kernel may reach another device: no remote copies, remote signals or barrier semaphores. Data moves between devices by JAX's collectives and lax.ppermute only.
A program may use at most 64 MiB of HBM per device.

v0:
```python
import jax
import jax.numpy as jnp
from jax import lax
from jax.sharding import PartitionSpec as P

STEPS = 2
time_step_sq = 0.0625


def with_halo(cells, sides, width):
    for axis, dim in sides:
        count = lax.axis_size(axis)
        ends = count - 1
        head = lax.slice_in_dim(cells, 0, width, axis=dim)
        tail = lax.slice_in_dim(cells, cells.shape[dim] - width, cells.shape[dim], axis=dim)
        cells = jnp.concatenate(
            [
                lax.ppermute(tail, axis, [(i, (i + 1) % count) for i in range(ends)]),
                cells,
                lax.ppermute(head, axis, [((i + 1) % count, i) for i in range(ends)]),
            ],
            axis=dim,
        )
    return cells


def passed_along(value, axis, by):
    size = lax.axis_size(axis)
    pairs = [(i, i + by) for i in range(size) if 0 <= i + by < size]
    return lax.ppermute(value, axis, pairs)


def backward_diff(stress, axis):
    upper = stress[:, 1:, 1:, 1:]
    if axis == 1:
        lower = stress[:, :-1, 1:, 1:]
    elif axis == 2:
        lower = stress[:, 1:, :-1, 1:]
    else:
        lower = stress[:, 1:, 1:, :-1]
    return upper - lower


def stencil(padded, lame_pad, shear_pad):
    span_x = padded.shape[2] - 2
    span_y = padded.shape[3] - 2
    span_z = padded.shape[4] - 2
    anchor = padded[:, :, : span_x + 1, : span_y + 1, : span_z + 1]
    grad_x = padded[:, :, 1:, : span_y + 1, : span_z + 1] - anchor
    grad_y = padded[:, :, : span_x + 1, 1:, : span_z + 1] - anchor
    grad_z = padded[:, :, : span_x + 1, : span_y + 1, 1:] - anchor
    strain_xx = grad_x[:, 0]
    strain_yy = grad_y[:, 1]
    strain_zz = grad_z[:, 2]
    strain_xy = 0.5 * (grad_y[:, 0] + grad_x[:, 1])
    strain_xz = 0.5 * (grad_z[:, 0] + grad_x[:, 2])
    strain_yz = 0.5 * (grad_z[:, 1] + grad_y[:, 2])
    lame = lame_pad[: span_x + 1, : span_y + 1, : span_z + 1]
    shear = shear_pad[: span_x + 1, : span_y + 1, : span_z + 1]
    dilation = strain_xx + strain_yy + strain_zz
    stress_xx = lame * dilation + 2.0 * shear * strain_xx
    stress_yy = lame * dilation + 2.0 * shear * strain_yy
    stress_zz = lame * dilation + 2.0 * shear * strain_zz
    stress_xy = 2.0 * shear * strain_xy
    stress_xz = 2.0 * shear * strain_xz
    stress_yz = 2.0 * shear * strain_yz
    force_x = (
        backward_diff(stress_xx, 1) + backward_diff(stress_xy, 2) + backward_diff(stress_xz, 3)
    )
    force_y = (
        backward_diff(stress_xy, 1) + backward_diff(stress_yy, 2) + backward_diff(stress_yz, 3)
    )
    force_z = (
        backward_diff(stress_xz, 1) + backward_diff(stress_yz, 2) + backward_diff(stress_zz, 3)
    )
    force = jnp.stack([force_x, force_y, force_z], axis=1)
    strain = jnp.stack([strain_xx, strain_yy, strain_zz, strain_xy, strain_xz, strain_yz], axis=1)
    return (force, strain[:, :, 1:, 1:, 1:])


def faces(fields):
    count = fields.shape[0]
    flat = fields.reshape((count * 3,) + fields.shape[2:])
    grown = with_halo(flat, (("gx", 1), ("gy", 2)), 1)
    grown = jnp.pad(grown, ((0, 0), (0, 0), (0, 0), (1, 1)))
    return grown.reshape((count, 3) + grown.shape[1:])


def lower_rims(moduli):
    pairs, cells_x, cells_y, depth = moduli.shape
    from_x = passed_along(moduli[:, cells_x - 1 :], "gx", 1)
    from_y = passed_along(moduli[:, :, cells_y - 1 :], "gy", 1)
    corner = jnp.zeros((pairs, 1, 1, depth), jnp.float32)
    top_row = jnp.concatenate([corner, from_y], axis=1)
    rest = jnp.concatenate([from_x, moduli], axis=1)
    grown = jnp.concatenate([top_row, rest], axis=2)
    return jnp.pad(grown, ((0, 0), (0, 1), (0, 1), (1, 1)))


def locate(cells, start_x, start_y, start_z, width_y, depth, span_x, span_y, span_z):
    coord_x = cells // (width_y * depth) - start_x
    coord_y = cells // depth % width_y - start_y
    coord_z = cells % depth - start_z
    index_x = lax.broadcasted_iota(jnp.int32, (1, span_x, 1, 1), 1)
    index_y = lax.broadcasted_iota(jnp.int32, (1, 1, span_y, 1), 2)
    index_z = lax.broadcasted_iota(jnp.int32, (1, 1, 1, span_z), 3)
    found = (
        (index_x == coord_x[:, None, None, None])
        & (index_y == coord_y[:, None, None, None])
        & (index_z == coord_z[:, None, None, None])
    )
    return found.astype(jnp.float32)


def pick(trace, lags):
    positions = lax.broadcasted_iota(jnp.int32, (1, trace.shape[1]), 1)
    chosen = positions == lags[:, None]
    return jnp.sum(jnp.where(chosen[:, :, None], trace, 0.0), axis=1)


def advance(current, earlier, force, amplitudes, masks, buoyancy):
    source = amplitudes[:, :, None, None, None] * masks[:, None]
    return 2.0 * current - earlier + time_step_sq * buoyancy * (force + source)


def correlate(master, strains, totals):
    weights = jnp.array([1.0, 1.0, 1.0, 2.0, 2.0, 2.0], jnp.float32)[:, None, None, None]
    summed = jnp.sum(strains, axis=0)
    dilation_term = (master[0] + master[1] + master[2]) * (summed[0] + summed[1] + summed[2])
    shear_term = 2.0 * jnp.sum(weights * master * summed, axis=0)
    return totals + jnp.stack([dilation_term, shear_term])


def local(
    fwd_now,
    fwd_prev,
    adj_now,
    adj_prev,
    lame_first,
    shear_mod,
    buoyancy,
    master_cell,
    master_lag,
    master_trace,
    receiver_cell,
    receiver_lag,
    receiver_trace,
):
    cells_x, cells_y, depth = lame_first.shape
    groups = lax.axis_size("grp")
    receivers = adj_now.shape[0]
    width_y = cells_y * lax.axis_size("gy")
    start_x = lax.axis_index("gx") * cells_x
    start_y = lax.axis_index("gy") * cells_y
    moduli = lower_rims(jnp.stack([lame_first, shear_mod]))
    lame_pad = moduli[0]
    shear_pad = moduli[1]
    receiver_masks = locate(
        receiver_cell, start_x, start_y, 0, width_y, depth, cells_x, cells_y, depth
    )
    receiver_amps = [pick(receiver_trace, receiver_lag + instant) for instant in range(STEPS)]
    master_amps = [pick(master_trace[None], master_lag + instant) for instant in range(STEPS)]
    totals = jnp.zeros((2, cells_x, cells_y, depth), jnp.float32)
    share = depth // groups
    z_start = lax.axis_index("grp") * share
    master_now = lax.dynamic_slice_in_dim(fwd_now, z_start, share, 3)
    master_prev = lax.dynamic_slice_in_dim(fwd_prev, z_start, share, 3)
    lame_share = lax.dynamic_slice_in_dim(lame_pad, z_start, share + 2, 2)
    shear_share = lax.dynamic_slice_in_dim(shear_pad, z_start, share + 2, 2)
    buoyancy_share = lax.dynamic_slice_in_dim(buoyancy, z_start, share, 2)
    master_mask = locate(
        master_cell, start_x, start_y, z_start, width_y, depth, cells_x, cells_y, share
    )
    adjoint = adj_now
    adjoint_prev = adj_prev
    for instant in range(STEPS):
        grown = with_halo(master_now, (("grp", 3), ("gx", 1), ("gy", 2)), 1)
        master_force, master_strain = stencil(grown[None], lame_share, shear_share)
        master_whole = lax.all_gather(master_strain[0], "grp", axis=3, tiled=True)
        if instant + 1 < STEPS:
            master_next = advance(
                master_now[None],
                master_prev[None],
                master_force,
                master_amps[instant],
                master_mask,
                buoyancy_share,
            )[0]
            master_prev, master_now = (master_now, master_next)
        padded = faces(adjoint)
        force, strain = stencil(padded, lame_pad, shear_pad)
        totals = correlate(master_whole, strain, totals)
        adjoint_next = advance(
            adjoint, adjoint_prev, force, receiver_amps[instant], receiver_masks, buoyancy
        )
        adjoint_prev, adjoint = (adjoint, adjoint_next)
    scale_out = 1.0 / (STEPS * receivers * groups)
    kernels = lax.psum_scatter(totals * scale_out, "grp", scatter_dimension=3, tiled=True)
    return (adjoint, kernels)


def solution(mesh):
    in_specs = (
        P(None, "gx", "gy", None),
        P(None, "gx", "gy", None),
        P("grp", None, "gx", "gy", None),
        P("grp", None, "gx", "gy", None),
        P("gx", "gy", None),
        P("gx", "gy", None),
        P("gx", "gy", None),
        P(),
        P(),
        P(),
        P("grp"),
        P("grp"),
        P("grp", None, None),
    )
    out_specs = (P("grp", None, "gx", "gy", None), P(None, "gx", "gy", "grp"))
    return jax.shard_map(local, mesh=mesh, in_specs=in_specs, out_specs=out_specs, check_vma=False)
```

profile of v0, /device:TPU:8, one launch (start us, length us, event | category | flops | bytes accessed | tf_op | source)
XLA Modules:
  0.0 201.1 jit_solution(10094206814735372614)
XLA Ops:
  7.2 0.7 copy_bitcast_fusion
  8.0 1.7 collective-permute-start
  9.7 3.5 %collective-permute-start.1 = (f32[2,1,8,128]{3,1,2,0:T(1,128)S(1)}, f32[2,1,8,128]{3,1,2,0:T(1,128)S(1)}, u32[]{:S(2)}, u32[]{:S(2)}) collective-permute-start(f32[2,1,8,128]{3,1,2,0:T(1,128)S(1)} %pad_maximum_fusion.14), channel_id=1, source_target_pairs={{0,8},{8,16},{16,24},{24,32},{32,40},{40,48},{48,56},{56,64},{64,7... | collective-permute-start | bytes 24584 | tf_op jit(solution)/shard_map/ppermute | solution.py:30
  13.2 1.0 constant_dynamic-slice_fusion.1
  14.2 3.4 %collective-permute-start.10 = (f32[3,4,8,1]{3,2,1,0:T(8,128)S(1)}, f32[3,4,8,1]{3,2,1,0:T(8,128)S(1)}, u32[]{:S(2)}, u32[]{:S(2)}) collective-permute-start(f32[3,4,8,1]{3,2,1,0:T(8,128)S(1)} %get-tuple-element.92), channel_id=1, source_target_pairs={{0,128},{128,256},{256,384},{1,129},{129,257},{257,385},{2,130},{1... | collective-permute-start | bytes 1160 | tf_op jit(solution)/shard_map/ppermute | solution.py:18
  17.6 1.3 collective-permute-start.11
  18.9 1.0 copy.414
  20.0 3.5 %collective-permute-start.2 = (f32[12,1,8,128]{3,1,2,0:T(1,128)S(1)}, f32[12,1,8,128]{3,1,2,0:T(1,128)S(1)}, u32[]{:S(2)}, u32[]{:S(2)}) collective-permute-start(f32[12,1,8,128]{3,1,2,0:T(1,128)S(1)} %get-tuple-element.66), channel_id=1, source_target_pairs={{0,8},{8,16},{16,24},{24,32},{32,40},{40,48},{48,56},{56,64},{64,7... | collective-permute-start | bytes 147464 | tf_op jit(solution)/shard_map/ppermute | solution.py:18
  24.2 0.9 constant_dynamic-slice_fusion.2
  25.8 0.7 fusion.74
  26.7 0.7 iota_compare_fusion.5
  27.4 0.7 broadcast_multiply_fusion.1
  28.4 0.8 select_reduce_fusion
  29.2 0.8 dynamic-slice_multiply_fusion
  30.8 4.7 %collective-permute-start.12 = (f32[3,1,8,34]{3,2,1,0:T(8,128)S(1)}, f32[3,1,8,34]{3,2,1,0:T(8,128)S(1)}, u32[]{:S(2)}, u32[]{:S(2)}) collective-permute-start(f32[3,1,8,34]{3,2,1,0:T(8,128)S(1)} %get-tuple-element.70), channel_id=1, source_target_pairs={{0,8},{8,16},{16,24},{24,32},{32,40},{40,48},{48,56},{56,64},{64,7... | collective-permute-start | bytes 9800 | tf_op jit(solution)/shard_map/ppermute | solution.py:18
  35.5 1.9 collective-permute-start.13
  37.4 3.6 %collective-permute-done.13 = f32[3,1,8,34]{3,2,1,0:T(8,128)S(1)} collective-permute-done((f32[3,1,8,34]{3,2,1,0:T(8,128)S(1)}, f32[3,1,8,34]{3,2,1,0:T(8,128)S(1)}, u32[]{:S(2)}, u32[]{:S(2)}) %collective-permute-start.13) | collective-permute-done | bytes 3296 | tf_op jit(solution)/shard_map/ppermute | solution.py:20
  41.2 2.4 %collective-permute-start.14 = (f32[3,6,1,34]{3,1,2,0:T(8,128)S(1)}, f32[3,6,1,34]{3,1,2,0:T(8,128)S(1)}, u32[]{:S(2)}, u32[]{:S(2)}) collective-permute-start(f32[3,6,1,34]{3,1,2,0:T(8,128)S(1)} %get-tuple-element.80), channel_id=1, source_target_pairs={{0,1},{1,2},{2,3},{3,4},{4,5},{5,6},{6,7},{8,9},{9,10},{10,11},{11... | collective-permute-start | bytes 7352 | tf_op jit(solution)/shard_map/ppermute | solution.py:18
  43.7 1.3 collective-permute-start.15
  45.1 2.2 %collective-permute-start.3 = (f32[12,1,8,128]{3,1,2,0:T(1,128)S(1)}, f32[12,1,8,128]{3,1,2,0:T(1,128)S(1)}, u32[]{:S(2)}, u32[]{:S(2)}) collective-permute-start(f32[12,1,8,128]{3,1,2,0:T(1,128)S(1)} %get-tuple-element.67), channel_id=1, source_target_pairs={{8,0},{16,8},{24,16},{32,24},{40,32},{48,40},{56,48},{64,56},{72,6... | collective-permute-start | bytes 147464 | tf_op jit(solution)/shard_map/ppermute | solution.py:20
  47.3 1.2 collective-permute-done.15
  49.6 4.6 %collective-permute-start.16 = (f32[3,4,8,1]{3,2,1,0:T(8,128)S(1)}, f32[3,4,8,1]{3,2,1,0:T(8,128)S(1)}, u32[]{:S(2)}, u32[]{:S(2)}) collective-permute-start(f32[3,4,8,1]{3,2,1,0:T(8,128)S(1)} %get-tuple-element.90), channel_id=1, source_target_pairs={{0,128},{128,256},{256,384},{1,129},{129,257},{257,385},{2,130},{1... | collective-permute-start | bytes 1160 | tf_op jit(solution)/shard_map/ppermute | solution.py:18
  54.1 1.3 collective-permute-start.17
  55.9 4.3 %collective-permute-done.17 = f32[3,4,8,1]{3,2,1,0:T(8,128)S(1)} collective-permute-done((f32[3,4,8,1]{3,2,1,0:T(8,128)S(1)}, f32[3,4,8,1]{3,2,1,0:T(8,128)S(1)}, u32[]{:S(2)}, u32[]{:S(2)}) %collective-permute-start.17) | collective-permute-done | bytes 416 | tf_op jit(solution)/shard_map/ppermute | solution.py:20
  60.2 2.6 %collective-permute-start.18 = (f32[3,1,8,34]{3,2,1,0:T(8,128)S(1)}, f32[3,1,8,34]{3,2,1,0:T(8,128)S(1)}, u32[]{:S(2)}, u32[]{:S(2)}) collective-permute-start(f32[3,1,8,34]{3,2,1,0:T(8,128)S(1)} %get-tuple-element.68), channel_id=1, source_target_pairs={{0,8},{8,16},{16,24},{24,32},{32,40},{40,48},{48,56},{56,64},{64,7... | collective-permute-start | bytes 9800 | tf_op jit(solution)/shard_map/ppermute | solution.py:18
  62.8 3.3 %collective-permute-start.19 = (f32[3,1,8,34]{3,2,1,0:T(8,128)S(1)}, f32[3,1,8,34]{3,2,1,0:T(8,128)S(1)}, u32[]{:S(2)}, u32[]{:S(2)}) collective-permute-start(f32[3,1,8,34]{3,2,1,0:T(8,128)S(1)} %get-tuple-element.69), channel_id=1, source_target_pairs={{8,0},{16,8},{24,16},{32,24},{40,32},{48,40},{56,48},{64,56},{72,6... | collective-permute-start | bytes 9800 | tf_op jit(solution)/shard_map/ppermute | solution.py:20
  66.1 17.6 %all-gather = f32[1,6,4,8,128]{3,2,1,0,4:T(4,128)S(1)} all-gather(f32[1,6,4,8,32]{3,2,1,0,4:T(4,128)S(1)} %copy.434), channel_id=2, replica_groups=mesh['grp'=4,'gx'=16,'gy'=8] {'grp'}, dimensions={4}, use_global_device_ids=true | all-gather | bytes 122880 | tf_op jit(solution)/shard_map/all_gather | solution.py:179
  84.4 1.5 collective-permute-start.20
  85.9 1.3 collective-permute-start.21
  87.3 5.0 %collective-permute-done.21 = f32[3,6,1,34]{3,1,2,0:T(8,128)S(1)} collective-permute-done((f32[3,6,1,34]{3,1,2,0:T(8,128)S(1)}, f32[3,6,1,34]{3,1,2,0:T(8,128)S(1)}, u32[]{:S(2)}, u32[]{:S(2)}) %collective-permute-start.21) | collective-permute-done | bytes 2480 | tf_op jit(solution)/shard_map/ppermute | solution.py:20
  92.9 4.3 %collective-permute-start.4 = (f32[12,6,1,128]{3,1,2,0:T(8,128)S(1)}, f32[12,6,1,128]{3,1,2,0:T(8,128)S(1)}, u32[]{:S(2)}, u32[]{:S(2)}) collective-permute-start(f32[12,6,1,128]{3,1,2,0:T(8,128)S(1)} %get-tuple-element.59), channel_id=1, source_target_pairs={{0,1},{1,2},{2,3},{3,4},{4,5},{5,6},{6,7},{8,9},{9,10},{10,11},{11... | collective-permute-start | bytes 110600 | tf_op jit(solution)/shard_map/ppermute | solution.py:18
  97.3 1.3 collective-permute-start.5
  98.6 18.0 %all-gather.1 = f32[1,6,4,8,128]{3,2,1,0,4:T(4,128)S(1)} all-gather(f32[1,6,4,8,32]{3,2,1,0,4:T(4,128)S(1)} %copy.451), channel_id=3, replica_groups=mesh['grp'=4,'gx'=16,'gy'=8] {'grp'}, dimensions={4}, use_global_device_ids=true | all-gather | bytes 122880 | tf_op jit(solution)/shard_map/all_gather | solution.py:179
  116.6 1.2 copy.452
  117.9 0.7 select_maximum_fusion.4
  120.7 3.5 %collective-permute-start.6 = (f32[12,1,8,128]{3,2,1,0:T(8,128)S(1)}, f32[12,1,8,128]{3,2,1,0:T(8,128)S(1)}, u32[]{:S(2)}, u32[]{:S(2)}) collective-permute-start(f32[12,1,8,128]{3,2,1,0:T(8,128)S(1)} %get-tuple-element.64), channel_id=1, source_target_pairs={{0,8},{8,16},{16,24},{24,32},{32,40},{40,48},{48,56},{56,64},{64,7... | collective-permute-start | bytes 147464 | tf_op jit(solution)/shard_map/ppermute | solution.py:18
  124.2 2.4 %collective-permute-start.7 = (f32[12,1,8,128]{3,2,1,0:T(8,128)S(1)}, f32[12,1,8,128]{3,2,1,0:T(8,128)S(1)}, u32[]{:S(2)}, u32[]{:S(2)}) collective-permute-start(f32[12,1,8,128]{3,2,1,0:T(8,128)S(1)} %get-tuple-element.65), channel_id=1, source_target_pairs={{8,0},{16,8},{24,16},{32,24},{40,32},{48,40},{56,48},{64,56},{72,6... | collective-permute-start | bytes 147464 | tf_op jit(solution)/shard_map/ppermute | solution.py:20
  127.2 4.8 %collective-permute-done.7 = f32[12,1,8,128]{3,2,1,0:T(8,128)S(1)} collective-permute-done((f32[12,1,8,128]{3,2,1,0:T(8,128)S(1)}, f32[12,1,8,128]{3,2,1,0:T(8,128)S(1)}, u32[]{:S(2)}, u32[]{:S(2)}) %collective-permute-start.7) | collective-permute-done | bytes 49184 | tf_op jit(solution)/shard_map/ppermute | solution.py:20
  132.0 1.3 collective-permute-start.8
  133.3 1.5 collective-permute-start.9
  134.8 3.6 %collective-permute-done.9 = f32[12,6,1,128]{3,2,1,0:T(1,128)S(1)} collective-permute-done((f32[12,6,1,128]{3,2,1,0:T(1,128)S(1)}, f32[12,6,1,128]{3,2,1,0:T(1,128)S(1)}, u32[]{:S(2)}, u32[]{:S(2)}) %collective-permute-start.9) | collective-permute-done | bytes 36896 | tf_op jit(solution)/shard_map/ppermute | solution.py:20
  138.4 0.7 select_maximum_fusion
  139.7 2.0 %copy_subtract_fusion.1 = (f32[4,3,5,9,129]{4,2,3,0,1:T(8,128)S(1)}, f32[4,3,5,9,129]{4,2,3,0,1:T(8,128)S(1)}, f32[4,3,5,9,129]{4,2,3,0,1:T(8,128)S(1)}) fusion(f32[4,3,5,9,129]{4,3,2,1,0:T(8,128)S(1)} %get-tuple-element.34, f32[4,3,5,9,129]{4,3,2,1,0:T(8,128)S(1)} %get-tuple-element.35, f32[4,3,5,9,129]{4,3,2,1,0:T(8,128)S(1)} %get-tuple-element.37, ...), kind=kLoop, calls=%fused_computation.16 | loop fusion | flops 208980 | bytes 1950480 | tf_op jit(solution)/shard_map/sub | solution.py:50
  143.4 1.0 reshape.361
  145.1 0.7 copy.463
  145.8 46.9 %reduce-scatter.4.cloned.1.call-done = f32[32,64]{1,0:T(8,128)} async-done(((f32[128,64]{1,0:T(8,128)}), f32[32,64]{1,0:T(8,128)}) %reduce-scatter.4.cloned.1.call-update) | async-done | bytes 8208
  192.6 0.8 reshape.362
  193.5 0.7 copy.465
  (132 shorter events, 9.9 us)
Async XLA Ops:
  7.2 37.8 %copy-start.7 = (f32[256,3]{0,1:T(4,128)S(1)}, f32[256,3]{0,1:T(4,128)}, u32[]{:S(2)}) copy-start(f32[256,3]{0,1:T(4,128)} %param.24) | copy-start | bytes 9220
  7.2 185.5 %reduce-scatter.4.cloned.1.call-start = ((), (), s32[]{:S(2)}) async-start(), calls=%async_computation.1 | async-start | bytes 81920
  8.0 40.8 %collective-permute-start = (f32[2,4,1,128]{3,1,2,0:T(4,128)S(1)}, f32[2,4,1,128]{3,1,2,0:T(4,128)S(1)}, u32[]{:S(2)}, u32[]{:S(2)}) collective-permute-start(f32[2,4,1,128]{3,1,2,0:T(4,128)S(1)} %pad_maximum_fusion.15), channel_id=1, source_target_pairs={{0,1},{1,2},{2,3},{3,4},{4,5},{5,6},{6,7},{8,9},{9,10},{10,11},{11... | collective-permute-start | bytes 12296 | tf_op jit(solution)/shard_map/ppermute | solution.py:30
  9.7 39.0 %collective-permute-start.1 = (f32[2,1,8,128]{3,1,2,0:T(1,128)S(1)}, f32[2,1,8,128]{3,1,2,0:T(1,128)S(1)}, u32[]{:S(2)}, u32[]{:S(2)}) collective-permute-start(f32[2,1,8,128]{3,1,2,0:T(1,128)S(1)} %pad_maximum_fusion.14), channel_id=1, source_target_pairs={{0,8},{8,16},{16,24},{24,32},{32,40},{40,48},{48,56},{56,64},{64,7... | collective-permute-start | bytes 24584 | tf_op jit(solution)/shard_map/ppermute | solution.py:30
  14.2 16.5 %collective-permute-start.10 = (f32[3,4,8,1]{3,2,1,0:T(8,128)S(1)}, f32[3,4,8,1]{3,2,1,0:T(8,128)S(1)}, u32[]{:S(2)}, u32[]{:S(2)}) collective-permute-start(f32[3,4,8,1]{3,2,1,0:T(8,128)S(1)} %get-tuple-element.92), channel_id=1, source_target_pairs={{0,128},{128,256},{256,384},{1,129},{129,257},{257,385},{2,130},{1... | collective-permute-start | bytes 1160 | tf_op jit(solution)/shard_map/ppermute | solution.py:18
  17.6 13.1 %collective-permute-start.11 = (f32[3,4,8,1]{3,2,1,0:T(8,128)S(1)}, f32[3,4,8,1]{3,2,1,0:T(8,128)S(1)}, u32[]{:S(2)}, u32[]{:S(2)}) collective-permute-start(f32[3,4,8,1]{3,2,1,0:T(8,128)S(1)} %get-tuple-element.93), channel_id=1, source_target_pairs={{128,0},{256,128},{384,256},{129,1},{257,129},{385,257},{130,2},{2... | collective-permute-start | bytes 1160 | tf_op jit(solution)/shard_map/ppermute | solution.py:20
  20.0 72.9 %collective-permute-start.2 = (f32[12,1,8,128]{3,1,2,0:T(1,128)S(1)}, f32[12,1,8,128]{3,1,2,0:T(1,128)S(1)}, u32[]{:S(2)}, u32[]{:S(2)}) collective-permute-start(f32[12,1,8,128]{3,1,2,0:T(1,128)S(1)} %get-tuple-element.66), channel_id=1, source_target_pairs={{0,8},{8,16},{16,24},{24,32},{32,40},{40,48},{48,56},{56,64},{64,7... | collective-permute-start | bytes 147464 | tf_op jit(solution)/shard_map/ppermute | solution.py:18
  30.8 6.6 %collective-permute-start.12 = (f32[3,1,8,34]{3,2,1,0:T(8,128)S(1)}, f32[3,1,8,34]{3,2,1,0:T(8,128)S(1)}, u32[]{:S(2)}, u32[]{:S(2)}) collective-permute-start(f32[3,1,8,34]{3,2,1,0:T(8,128)S(1)} %get-tuple-element.70), channel_id=1, source_target_pairs={{0,8},{8,16},{16,24},{24,32},{32,40},{40,48},{48,56},{56,64},{64,7... | collective-permute-start | bytes 9800 | tf_op jit(solution)/shard_map/ppermute | solution.py:18
  35.5 5.6 %collective-permute-start.13 = (f32[3,1,8,34]{3,2,1,0:T(8,128)S(1)}, f32[3,1,8,34]{3,2,1,0:T(8,128)S(1)}, u32[]{:S(2)}, u32[]{:S(2)}) collective-permute-start(f32[3,1,8,34]{3,2,1,0:T(8,128)S(1)} %get-tuple-element.71), channel_id=1, source_target_pairs={{8,0},{16,8},{24,16},{32,24},{40,32},{48,40},{56,48},{64,56},{72,6... | collective-permute-start | bytes 9800 | tf_op jit(solution)/shard_map/ppermute | solution.py:20
  41.2 8.2 %copy-start.1 = (f32[3,4,8,128]{3,2,1,0:T(8,128)S(1)}, f32[3,4,8,128]{3,2,1,0:T(8,128)}, u32[]{:S(2)}) copy-start(f32[3,4,8,128]{3,2,1,0:T(8,128)} %param.15) | copy-start | bytes 147460
  41.2 8.2 %copy-start.6 = (f32[3,4,8,128]{3,2,1,0:T(8,128)S(1)}, f32[3,4,8,128]{3,2,1,0:T(8,128)}, u32[]{:S(2)}) copy-start(f32[3,4,8,128]{3,2,1,0:T(8,128)} %param.16) | copy-start | bytes 147460
  41.2 3.9 %collective-permute-start.14 = (f32[3,6,1,34]{3,1,2,0:T(8,128)S(1)}, f32[3,6,1,34]{3,1,2,0:T(8,128)S(1)}, u32[]{:S(2)}, u32[]{:S(2)}) collective-permute-start(f32[3,6,1,34]{3,1,2,0:T(8,128)S(1)} %get-tuple-element.80), channel_id=1, source_target_pairs={{0,1},{1,2},{2,3},{3,4},{4,5},{5,6},{6,7},{8,9},{9,10},{10,11},{11... | collective-permute-start | bytes 7352 | tf_op jit(solution)/shard_map/ppermute | solution.py:18
  43.7 4.9 %collective-permute-start.15 = (f32[3,6,1,34]{3,1,2,0:T(8,128)S(1)}, f32[3,6,1,34]{3,1,2,0:T(8,128)S(1)}, u32[]{:S(2)}, u32[]{:S(2)}) collective-permute-start(f32[3,6,1,34]{3,1,2,0:T(8,128)S(1)} %get-tuple-element.81), channel_id=1, source_target_pairs={{1,0},{2,1},{3,2},{4,3},{5,4},{6,5},{7,6},{9,8},{10,9},{11,10},{12... | collective-permute-start | bytes 7352 | tf_op jit(solution)/shard_map/ppermute | solution.py:20
  45.1 47.8 %collective-permute-start.3 = (f32[12,1,8,128]{3,1,2,0:T(1,128)S(1)}, f32[12,1,8,128]{3,1,2,0:T(1,128)S(1)}, u32[]{:S(2)}, u32[]{:S(2)}) collective-permute-start(f32[12,1,8,128]{3,1,2,0:T(1,128)S(1)} %get-tuple-element.67), channel_id=1, source_target_pairs={{8,0},{16,8},{24,16},{32,24},{40,32},{48,40},{56,48},{64,56},{72,6... | collective-permute-start | bytes 147464 | tf_op jit(solution)/shard_map/ppermute | solution.py:20
  49.6 6.3 %collective-permute-start.16 = (f32[3,4,8,1]{3,2,1,0:T(8,128)S(1)}, f32[3,4,8,1]{3,2,1,0:T(8,128)S(1)}, u32[]{:S(2)}, u32[]{:S(2)}) collective-permute-start(f32[3,4,8,1]{3,2,1,0:T(8,128)S(1)} %get-tuple-element.90), channel_id=1, source_target_pairs={{0,128},{128,256},{256,384},{1,129},{129,257},{257,385},{2,130},{1... | collective-permute-start | bytes 1160 | tf_op jit(solution)/shard_map/ppermute | solution.py:18
  54.1 6.0 %collective-permute-start.17 = (f32[3,4,8,1]{3,2,1,0:T(8,128)S(1)}, f32[3,4,8,1]{3,2,1,0:T(8,128)S(1)}, u32[]{:S(2)}, u32[]{:S(2)}) collective-permute-start(f32[3,4,8,1]{3,2,1,0:T(8,128)S(1)} %get-tuple-element.91), channel_id=1, source_target_pairs={{128,0},{256,128},{384,256},{129,1},{257,129},{385,257},{130,2},{2... | collective-permute-start | bytes 1160 | tf_op jit(solution)/shard_map/ppermute | solution.py:20
  60.2 24.1 %collective-permute-start.18 = (f32[3,1,8,34]{3,2,1,0:T(8,128)S(1)}, f32[3,1,8,34]{3,2,1,0:T(8,128)S(1)}, u32[]{:S(2)}, u32[]{:S(2)}) collective-permute-start(f32[3,1,8,34]{3,2,1,0:T(8,128)S(1)} %get-tuple-element.68), channel_id=1, source_target_pairs={{0,8},{8,16},{16,24},{24,32},{32,40},{40,48},{48,56},{56,64},{64,7... | collective-permute-start | bytes 9800 | tf_op jit(solution)/shard_map/ppermute | solution.py:18
  62.8 21.5 %collective-permute-start.19 = (f32[3,1,8,34]{3,2,1,0:T(8,128)S(1)}, f32[3,1,8,34]{3,2,1,0:T(8,128)S(1)}, u32[]{:S(2)}, u32[]{:S(2)}) collective-permute-start(f32[3,1,8,34]{3,2,1,0:T(8,128)S(1)} %get-tuple-element.69), channel_id=1, source_target_pairs={{8,0},{16,8},{24,16},{32,24},{40,32},{48,40},{56,48},{64,56},{72,6... | collective-permute-start | bytes 9800 | tf_op jit(solution)/shard_map/ppermute | solution.py:20
  84.3 50.5 %copy-start.2 = (f32[1,6,4,8,128]{4,2,3,1,0:T(4,128)}, f32[1,6,4,8,128]{4,2,3,1,0:T(4,128)S(1)}, u32[]{:S(2)}) copy-start(f32[1,6,4,8,128]{4,2,3,1,0:T(4,128)S(1)} %copy.435) | copy-start | bytes 294916
  84.4 2.8 %collective-permute-start.20 = (f32[3,6,1,34]{3,1,2,0:T(8,128)S(1)}, f32[3,6,1,34]{3,1,2,0:T(8,128)S(1)}, u32[]{:S(2)}, u32[]{:S(2)}) collective-permute-start(f32[3,6,1,34]{3,1,2,0:T(8,128)S(1)} %get-tuple-element.78), channel_id=1, source_target_pairs={{0,1},{1,2},{2,3},{3,4},{4,5},{5,6},{6,7},{8,9},{9,10},{10,11},{11... | collective-permute-start | bytes 7352 | tf_op jit(solution)/shard_map/ppermute | solution.py:18
  85.9 6.4 %collective-permute-start.21 = (f32[3,6,1,34]{3,1,2,0:T(8,128)S(1)}, f32[3,6,1,34]{3,1,2,0:T(8,128)S(1)}, u32[]{:S(2)}, u32[]{:S(2)}) collective-permute-start(f32[3,6,1,34]{3,1,2,0:T(8,128)S(1)} %get-tuple-element.79), channel_id=1, source_target_pairs={{1,0},{2,1},{3,2},{4,3},{5,4},{6,5},{7,6},{9,8},{10,9},{11,10},{12... | collective-permute-start | bytes 7352 | tf_op jit(solution)/shard_map/ppermute | solution.py:20
  92.9 24.9 %collective-permute-start.4 = (f32[12,6,1,128]{3,1,2,0:T(8,128)S(1)}, f32[12,6,1,128]{3,1,2,0:T(8,128)S(1)}, u32[]{:S(2)}, u32[]{:S(2)}) collective-permute-start(f32[12,6,1,128]{3,1,2,0:T(8,128)S(1)} %get-tuple-element.59), channel_id=1, source_target_pairs={{0,1},{1,2},{2,3},{3,4},{4,5},{5,6},{6,7},{8,9},{9,10},{10,11},{11... | collective-permute-start | bytes 110600 | tf_op jit(solution)/shard_map/ppermute | solution.py:18
  97.3 20.6 %collective-permute-start.5 = (f32[12,6,1,128]{3,1,2,0:T(8,128)S(1)}, f32[12,6,1,128]{3,1,2,0:T(8,128)S(1)}, u32[]{:S(2)}, u32[]{:S(2)}) collective-permute-start(f32[12,6,1,128]{3,1,2,0:T(8,128)S(1)} %get-tuple-element.60), channel_id=1, source_target_pairs={{1,0},{2,1},{3,2},{4,3},{5,4},{6,5},{7,6},{9,8},{10,9},{11,10},{12... | collective-permute-start | bytes 110600 | tf_op jit(solution)/shard_map/ppermute | solution.py:20
  119.5 0.9 copy-start
  119.5 1.0 copy-start.5
  120.7 6.5 %collective-permute-start.6 = (f32[12,1,8,128]{3,2,1,0:T(8,128)S(1)}, f32[12,1,8,128]{3,2,1,0:T(8,128)S(1)}, u32[]{:S(2)}, u32[]{:S(2)}) collective-permute-start(f32[12,1,8,128]{3,2,1,0:T(8,128)S(1)} %get-tuple-element.64), channel_id=1, source_target_pairs={{0,8},{8,16},{16,24},{24,32},{32,40},{40,48},{48,56},{56,64},{64,7... | collective-permute-start | bytes 147464 | tf_op jit(solution)/shard_map/ppermute | solution.py:18
  124.2 7.8 %collective-permute-start.7 = (f32[12,1,8,128]{3,2,1,0:T(8,128)S(1)}, f32[12,1,8,128]{3,2,1,0:T(8,128)S(1)}, u32[]{:S(2)}, u32[]{:S(2)}) collective-permute-start(f32[12,1,8,128]{3,2,1,0:T(8,128)S(1)} %get-tuple-element.65), channel_id=1, source_target_pairs={{8,0},{16,8},{24,16},{32,24},{40,32},{48,40},{56,48},{64,56},{72,6... | collective-permute-start | bytes 147464 | tf_op jit(solution)/shard_map/ppermute | solution.py:20
  132.0 2.8 %collective-permute-start.8 = (f32[12,6,1,128]{3,2,1,0:T(1,128)S(1)}, f32[12,6,1,128]{3,2,1,0:T(1,128)S(1)}, u32[]{:S(2)}, u32[]{:S(2)}) collective-permute-start(f32[12,6,1,128]{3,2,1,0:T(1,128)S(1)} %get-tuple-element.54), channel_id=1, source_target_pairs={{0,1},{1,2},{2,3},{3,4},{4,5},{5,6},{6,7},{8,9},{9,10},{10,11},{11... | collective-permute-start | bytes 110600 | tf_op jit(solution)/shard_map/ppermute | solution.py:18
  133.3 5.1 %collective-permute-start.9 = (f32[12,6,1,128]{3,2,1,0:T(1,128)S(1)}, f32[12,6,1,128]{3,2,1,0:T(1,128)S(1)}, u32[]{:S(2)}, u32[]{:S(2)}) collective-permute-start(f32[12,6,1,128]{3,2,1,0:T(1,128)S(1)} %get-tuple-element.55), channel_id=1, source_target_pairs={{1,0},{2,1},{3,2},{4,3},{5,4},{6,5},{7,6},{9,8},{10,9},{11,10},{12... | collective-permute-start | bytes 110600 | tf_op jit(solution)/shard_map/ppermute | solution.py:20
  142.0 0.9 copy-start.4
  142.1 0.9 copy-start.3
  142.1 0.9 copy-start.8
Sparse Core Ops, SparseCore 0:
  144.6 48.0 reduce-scatter.3
where the time goes:
time: 202 us; the launch traced here: 201 us
  waiting for transfers between devices  69.5 us (34%)
  starting transfers between devices  54.6 us (27%)
  blocking collectives  35.6 us (18%)
  between operations  16.4 us (8%)
  other arithmetic  13.2 us (7%)
  local copies, waits for them, and re-layouts  11.7 us (6%)
    unnamed x2, waiting for transfers between devices  46.9 us
    all_gather x2, blocking collectives, local(): master_whole = lax.all_gather(master_strain[0], 'grp', axis=3, tiled=True)  35.6 us
    ppermute x10, starting transfers between devices, with_halo(): lax.ppermute(tail, axis, [(i, (i + 1) % count) for i in range(ends)])  31.7 us
    ppermute x10, waiting for transfers between devices, with_halo(): lax.ppermute(head, axis, [((i + 1) % count, i) for i in range(ends)])  22.5 us
    ppermute x10, starting transfers between devices, with_halo(): lax.ppermute(head, axis, [((i + 1) % count, i) for i in range(ends)])  17.7 us
    unnamed x36, local copies, waits for them, and re-layouts  5.5 us
    ppermute x2, starting transfers between devices, passed_along(): return lax.ppermute(value, axis, pairs)  5.22 us
  transfers between devices with their start and end apart: 23, of which 8 were waited for; matrix products, arithmetic and copies ran while one was open for 7% of the time, Pallas kernels for 0%

commit v1 on v0

--- a/solution.py
+++ b/solution.py
@@ -176,7 +176,8 @@
     for instant in range(STEPS):
         grown = with_halo(master_now, (("grp", 3), ("gx", 1), ("gy", 2)), 1)
         master_force, master_strain = stencil(grown[None], lame_share, shear_share)
-        master_whole = lax.all_gather(master_strain[0], "grp", axis=3, tiled=True)
+        copies = jnp.concatenate([master_strain[0]] * lax.axis_size("grp"), axis=3)
+        master_whole = lax.all_to_all(copies, "grp", 3, 3, tiled=True)
         if instant + 1 < STEPS:
             master_next = advance(
                 master_now[None],

time: 202 us -> 190 us (0.941)
  blocking collectives: 35.6 us -> 0 us
  starting transfers between devices: 54.6 us -> 69.5 us
  local copies, waits for them, and re-layouts: 11.7 us -> 21.7 us
  waiting for transfers between devices: 69.5 us -> 65.5 us
  other arithmetic: 13.2 us -> 15.3 us
    all_gather x2 -> x0, blocking collectives: 35.6 us -> none  [local(): master_whole = lax.all_gather(master_strain[0], 'grp', axis=3, tiled=True)]
    unnamed x36 -> x38, local copies, waits for them, and re-layouts: 5.5 us -> 14.1 us
    all_to_all x0 -> x2, starting transfers between devices: none -> 8.52 us  [local(): master_whole = lax.all_to_all(copies, 'grp', 3, 3, tiled=True)]
    ppermute x10, starting transfers between devices: 31.7 us -> 38.6 us  [with_halo(): lax.ppermute(tail, axis, [(i, (i + 1) % count) for i in range(ends)])]
    ppermute x10, waiting for transfers between devices: 22.5 us -> 16.7 us  [with_halo(): lax.ppermute(head, axis, [((i + 1) % count, i) for i in range(ends)])]
  transfers between devices with their start and end apart: 23 -> 25, of which waited for: 8 -> 8; matrix products, arithmetic and copies ran while one was open for 7% -> 15% of each run, Pallas kernels for 0% -> 0%
where the time goes in v1:
time: 190 us; the launch traced here: 188 us
  starting transfers between devices  69.5 us (37%)
  waiting for transfers between devices  65.5 us (34%)
  local copies, waits for them, and re-layouts  21.7 us (11%)
  between operations  16.4 us (9%)
  other arithmetic  15.3 us (8%)
    unnamed x2, waiting for transfers between devices  48.5 us
    ppermute x10, starting transfers between devices, with_halo(): lax.ppermute(tail, axis, [(i, (i + 1) % count) for i in range(ends)])  38.6 us
    ppermute x10, starting transfers between devices, with_halo(): lax.ppermute(head, axis, [((i + 1) % count, i) for i in range(ends)])  17.2 us
    ppermute x10, waiting for transfers between devices, with_halo(): lax.ppermute(head, axis, [((i + 1) % count, i) for i in range(ends)])  16.7 us
    unnamed x38, local copies, waits for them, and re-layouts  14.1 us
    all_to_all x2, starting transfers between devices, local(): master_whole = lax.all_to_all(copies, 'grp', 3, 3, tiled=True)  8.52 us
    ppermute x2, starting transfers between devices, passed_along(): return lax.ppermute(value, axis, pairs)  5.22 us
  transfers between devices with their start and end apart: 25, of which 8 were waited for; matrix products, arithmetic and copies ran while one was open for 15% of the time, Pallas kernels for 0%

profile of v1, /device:TPU:8, one launch (start us, length us, event | category | flops | bytes accessed | tf_op | source)
XLA Modules:
  0.0 188.3 jit_solution(6874774887977721284)
XLA Ops:
  7.2 0.7 copy_bitcast_fusion
  7.9 1.7 collective-permute-start
  9.7 3.5 %collective-permute-start.1 = (f32[2,1,8,128]{3,1,2,0:T(1,128)S(1)}, f32[2,1,8,128]{3,1,2,0:T(1,128)S(1)}, u32[]{:S(2)}, u32[]{:S(2)}) collective-permute-start(f32[2,1,8,128]{3,1,2,0:T(1,128)S(1)} %pad_maximum_fusion.16), channel_id=1, source_target_pairs={{0,8},{8,16},{16,24},{24,32},{32,40},{40,48},{48,56},{56,64},{64,7... | collective-permute-start | bytes 24584 | tf_op jit(solution)/shard_map/ppermute | solution.py:30
  13.2 1.0 constant_dynamic-slice_fusion.1
  14.2 3.4 %collective-permute-start.10 = (f32[3,4,8,1]{3,2,1,0:T(8,128)S(1)}, f32[3,4,8,1]{3,2,1,0:T(8,128)S(1)}, u32[]{:S(2)}, u32[]{:S(2)}) collective-permute-start(f32[3,4,8,1]{3,2,1,0:T(8,128)S(1)} %get-tuple-element.101), channel_id=1, source_target_pairs={{0,128},{128,256},{256,384},{1,129},{129,257},{257,385},{2,130},{1... | collective-permute-start | bytes 1160 | tf_op jit(solution)/shard_map/ppermute | solution.py:18
  17.6 1.3 collective-permute-start.11
  18.9 1.0 copy.223
  19.9 3.5 %collective-permute-start.2 = (f32[12,1,8,128]{3,1,2,0:T(1,128)S(1)}, f32[12,1,8,128]{3,1,2,0:T(1,128)S(1)}, u32[]{:S(2)}, u32[]{:S(2)}) collective-permute-start(f32[12,1,8,128]{3,1,2,0:T(1,128)S(1)} %get-tuple-element.69), channel_id=1, source_target_pairs={{0,8},{8,16},{16,24},{24,32},{32,40},{40,48},{48,56},{56,64},{64,7... | collective-permute-start | bytes 147464 | tf_op jit(solution)/shard_map/ppermute | solution.py:18
  24.1 0.9 constant_dynamic-slice_fusion.2
  26.6 0.7 iota_compare_fusion.5
  28.4 0.8 select_reduce_fusion
  29.2 0.8 dynamic-slice_multiply_fusion
  30.8 4.7 %collective-permute-start.12 = (f32[3,1,8,34]{3,2,1,0:T(8,128)S(1)}, f32[3,1,8,34]{3,2,1,0:T(8,128)S(1)}, u32[]{:S(2)}, u32[]{:S(2)}) collective-permute-start(f32[3,1,8,34]{3,2,1,0:T(8,128)S(1)} %get-tuple-element.73), channel_id=1, source_target_pairs={{0,8},{8,16},{16,24},{24,32},{32,40},{40,48},{48,56},{56,64},{64,7... | collective-permute-start | bytes 9800 | tf_op jit(solution)/shard_map/ppermute | solution.py:18
  35.4 1.9 %collective-permute-start.13 = (f32[3,1,8,34]{3,2,1,0:T(8,128)S(1)}, f32[3,1,8,34]{3,2,1,0:T(8,128)S(1)}, u32[]{:S(2)}, u32[]{:S(2)}) collective-permute-start(f32[3,1,8,34]{3,2,1,0:T(8,128)S(1)} %get-tuple-element.74), channel_id=1, source_target_pairs={{8,0},{16,8},{24,16},{32,24},{40,32},{48,40},{56,48},{64,56},{72,6... | collective-permute-start | bytes 9800 | tf_op jit(solution)/shard_map/ppermute | solution.py:20
  37.4 3.6 %collective-permute-done.13 = f32[3,1,8,34]{3,2,1,0:T(8,128)S(1)} collective-permute-done((f32[3,1,8,34]{3,2,1,0:T(8,128)S(1)}, f32[3,1,8,34]{3,2,1,0:T(8,128)S(1)}, u32[]{:S(2)}, u32[]{:S(2)}) %collective-permute-start.13) | collective-permute-done | bytes 3296 | tf_op jit(solution)/shard_map/ppermute | solution.py:20
  41.2 2.3 %collective-permute-start.14 = (f32[3,6,1,34]{3,2,1,0:T(1,128)S(1)}, f32[3,6,1,34]{3,2,1,0:T(1,128)S(1)}, u32[]{:S(2)}, u32[]{:S(2)}) collective-permute-start(f32[3,6,1,34]{3,2,1,0:T(1,128)S(1)} %get-tuple-element.97), channel_id=1, source_target_pairs={{0,1},{1,2},{2,3},{3,4},{4,5},{5,6},{6,7},{8,9},{9,10},{10,11},{11... | collective-permute-start | bytes 7352 | tf_op jit(solution)/shard_map/ppermute | solution.py:18
  43.5 1.3 collective-permute-start.15
  45.0 2.3 %collective-permute-start.3 = (f32[12,1,8,128]{3,1,2,0:T(1,128)S(1)}, f32[12,1,8,128]{3,1,2,0:T(1,128)S(1)}, u32[]{:S(2)}, u32[]{:S(2)}) collective-permute-start(f32[12,1,8,128]{3,1,2,0:T(1,128)S(1)} %get-tuple-element.70), channel_id=1, source_target_pairs={{8,0},{16,8},{24,16},{32,24},{40,32},{48,40},{56,48},{64,56},{72,6... | collective-permute-start | bytes 147464 | tf_op jit(solution)/shard_map/ppermute | solution.py:20
  47.3 1.0 collective-permute-done.15
  49.4 4.6 %collective-permute-start.16 = (f32[3,4,8,1]{3,2,1,0:T(8,128)S(1)}, f32[3,4,8,1]{3,2,1,0:T(8,128)S(1)}, u32[]{:S(2)}, u32[]{:S(2)}) collective-permute-start(f32[3,4,8,1]{3,2,1,0:T(8,128)S(1)} %get-tuple-element.99), channel_id=1, source_target_pairs={{0,128},{128,256},{256,384},{1,129},{129,257},{257,385},{2,130},{1... | collective-permute-start | bytes 1160 | tf_op jit(solution)/shard_map/ppermute | solution.py:18
  54.0 1.3 collective-permute-start.17
  55.7 4.3 %collective-permute-done.17 = f32[3,4,8,1]{3,2,1,0:T(8,128)S(1)} collective-permute-done((f32[3,4,8,1]{3,2,1,0:T(8,128)S(1)}, f32[3,4,8,1]{3,2,1,0:T(8,128)S(1)}, u32[]{:S(2)}, u32[]{:S(2)}) %collective-permute-start.17) | collective-permute-done | bytes 416 | tf_op jit(solution)/shard_map/ppermute | solution.py:20
  60.1 2.6 %collective-permute-start.18 = (f32[3,1,8,34]{3,2,1,0:T(8,128)S(1)}, f32[3,1,8,34]{3,2,1,0:T(8,128)S(1)}, u32[]{:S(2)}, u32[]{:S(2)}) collective-permute-start(f32[3,1,8,34]{3,2,1,0:T(8,128)S(1)} %get-tuple-element.71), channel_id=1, source_target_pairs={{0,8},{8,16},{16,24},{24,32},{32,40},{40,48},{48,56},{56,64},{64,7... | collective-permute-start | bytes 9800 | tf_op jit(solution)/shard_map/ppermute | solution.py:18
  62.6 3.3 %collective-permute-start.19 = (f32[3,1,8,34]{3,2,1,0:T(8,128)S(1)}, f32[3,1,8,34]{3,2,1,0:T(8,128)S(1)}, u32[]{:S(2)}, u32[]{:S(2)}) collective-permute-start(f32[3,1,8,34]{3,2,1,0:T(8,128)S(1)} %get-tuple-element.72), channel_id=1, source_target_pairs={{8,0},{16,8},{24,16},{32,24},{40,32},{48,40},{56,48},{64,56},{72,6... | collective-permute-start | bytes 9800 | tf_op jit(solution)/shard_map/ppermute | solution.py:20
  66.2 2.1 %collective-permute-done.19 = f32[3,1,8,34]{3,2,1,0:T(8,128)S(1)} collective-permute-done((f32[3,1,8,34]{3,2,1,0:T(8,128)S(1)}, f32[3,1,8,34]{3,2,1,0:T(8,128)S(1)}, u32[]{:S(2)}, u32[]{:S(2)}) %collective-permute-start.19) | collective-permute-done | bytes 3296 | tf_op jit(solution)/shard_map/ppermute | solution.py:20
  68.5 2.0 %collective-permute-start.20 = (f32[3,6,1,34]{3,2,1,0:T(1,128)S(1)}, f32[3,6,1,34]{3,2,1,0:T(1,128)S(1)}, u32[]{:S(2)}, u32[]{:S(2)}) collective-permute-start(f32[3,6,1,34]{3,2,1,0:T(1,128)S(1)} %get-tuple-element.91), channel_id=1, source_target_pairs={{0,1},{1,2},{2,3},{3,4},{4,5},{5,6},{6,7},{8,9},{9,10},{10,11},{11... | collective-permute-start | bytes 7352 | tf_op jit(solution)/shard_map/ppermute | solution.py:18
  70.5 1.3 collective-permute-start.21
  72.7 2.4 %reshape.353 = f32[4,1,6144]{2,1,0:T(1,128)} reshape(f32[128,6,4,8]{3,2,1,0:T(4,128)S(1)} %bitcast.235) | data formatting | bytes 196608
  75.1 4.0 %all-to-all-start = ((f32[4,1,6144]{2,1,0:T(1,128)}), f32[4,1,6144]{2,1,0:T(1,128)S(1)}, u32[]{:S(2)}, u32[]{:S(2)}) async-start(f32[4,1,6144]{2,1,0:T(1,128)} %reshape.353), calls=%async_computation | async-start | bytes 196608 | tf_op jit(solution)/shard_map/all_to_all | solution.py:180
  79.9 6.8 %collective-permute-start.4 = (f32[12,6,1,128]{3,1,2,0:T(8,128)S(1)}, f32[12,6,1,128]{3,1,2,0:T(8,128)S(1)}, u32[]{:S(2)}, u32[]{:S(2)}) collective-permute-start(f32[12,6,1,128]{3,1,2,0:T(8,128)S(1)} %get-tuple-element.59), channel_id=1, source_target_pairs={{0,1},{1,2},{2,3},{3,4},{4,5},{5,6},{6,7},{8,9},{9,10},{10,11},{11... | collective-permute-start | bytes 110600 | tf_op jit(solution)/shard_map/ppermute | solution.py:18
  86.6 1.3 collective-permute-start.5
  88.8 2.4 %reshape.351 = f32[4,1,6144]{2,1,0:T(1,128)} reshape(f32[128,6,4,8]{3,2,1,0:T(4,128)S(1)} %bitcast.236) | data formatting | bytes 196608
  91.3 4.5 %all-to-all-start.1 = ((f32[4,1,6144]{2,1,0:T(1,128)}), f32[4,1,6144]{2,1,0:T(1,128)S(1)}, u32[]{:S(2)}, u32[]{:S(2)}) async-start(f32[4,1,6144]{2,1,0:T(1,128)} %reshape.351), calls=%async_computation.1 | async-start | bytes 196608 | tf_op jit(solution)/shard_map/all_to_all | solution.py:180
  96.3 0.9 reduce.3
  97.2 1.9 %reshape.354 = f32[128,6,4,8]{3,2,1,0:T(4,128)S(1)} reshape(f32[4,6144]{1,0:T(4,128)S(1)} %reduce.3) | data formatting | bytes 196608
  99.7 0.7 select_maximum_fusion.4
  102.6 5.4 %collective-permute-start.6 = (f32[12,1,8,128]{3,2,1,0:T(8,128)S(1)}, f32[12,1,8,128]{3,2,1,0:T(8,128)S(1)}, u32[]{:S(2)}, u32[]{:S(2)}) collective-permute-start(f32[12,1,8,128]{3,2,1,0:T(8,128)S(1)} %get-tuple-element.67), channel_id=1, source_target_pairs={{0,8},{8,16},{16,24},{24,32},{32,40},{40,48},{48,56},{56,64},{64,7... | collective-permute-start | bytes 147464 | tf_op jit(solution)/shard_map/ppermute | solution.py:18
  108.0 1.9 %collective-permute-start.7 = (f32[12,1,8,128]{3,2,1,0:T(8,128)S(1)}, f32[12,1,8,128]{3,2,1,0:T(8,128)S(1)}, u32[]{:S(2)}, u32[]{:S(2)}) collective-permute-start(f32[12,1,8,128]{3,2,1,0:T(8,128)S(1)} %get-tuple-element.68), channel_id=1, source_target_pairs={{8,0},{16,8},{24,16},{32,24},{40,32},{48,40},{56,48},{64,56},{72,6... | collective-permute-start | bytes 147464 | tf_op jit(solution)/shard_map/ppermute | solution.py:20
  110.5 4.6 %collective-permute-done.7 = f32[12,1,8,128]{3,2,1,0:T(8,128)S(1)} collective-permute-done((f32[12,1,8,128]{3,2,1,0:T(8,128)S(1)}, f32[12,1,8,128]{3,2,1,0:T(8,128)S(1)}, u32[]{:S(2)}, u32[]{:S(2)}) %collective-permute-start.7) | collective-permute-done | bytes 49184 | tf_op jit(solution)/shard_map/ppermute | solution.py:20
  115.2 3.4 %collective-permute-start.8 = (f32[12,6,1,128]{3,2,1,0:T(1,128)S(1)}, f32[12,6,1,128]{3,2,1,0:T(1,128)S(1)}, u32[]{:S(2)}, u32[]{:S(2)}) collective-permute-start(f32[12,6,1,128]{3,2,1,0:T(1,128)S(1)} %get-tuple-element.54), channel_id=1, source_target_pairs={{0,1},{1,2},{2,3},{3,4},{4,5},{5,6},{6,7},{8,9},{9,10},{10,11},{11... | collective-permute-start | bytes 110600 | tf_op jit(solution)/shard_map/ppermute | solution.py:18
  118.6 1.3 collective-permute-start.9
  119.9 0.9 reduce.2
  120.8 1.9 %reshape.352 = f32[128,6,4,8]{3,2,1,0:T(4,128)S(1)} reshape(f32[4,6144]{1,0:T(4,128)S(1)} %reduce.2) | data formatting | bytes 196608
  123.4 1.0 collective-permute-done.9
  125.6 2.0 %copy_subtract_fusion.1 = (f32[4,3,5,9,129]{4,2,3,0,1:T(8,128)S(1)}, f32[4,3,5,9,129]{4,2,3,0,1:T(8,128)S(1)}, f32[4,3,5,9,129]{4,2,3,0,1:T(8,128)S(1)}) fusion(f32[4,3,5,9,129]{4,3,2,1,0:T(8,128)S(1)} %get-tuple-element.34, f32[4,3,5,9,129]{4,3,2,1,0:T(8,128)S(1)} %get-tuple-element.35, f32[4,3,5,9,129]{4,3,2,1,0:T(8,128)S(1)} %get-tuple-element.37, ...), kind=kLoop, calls=%fused_computation.16 | loop fusion | flops 208980 | bytes 1950480 | tf_op jit(solution)/shard_map/sub | solution.py:50
  129.1 1.0 reshape.349
  131.4 48.5 %reduce-scatter.4.cloned.1.call-done = f32[32,64]{1,0:T(8,128)} async-done(((f32[128,64]{1,0:T(8,128)}), f32[32,64]{1,0:T(8,128)}) %reduce-scatter.4.cloned.1.call-update) | async-done | bytes 8208
  179.9 0.8 reshape.350
  (145 shorter events, 16.5 us)
Async XLA Ops:
  7.2 37.6 %copy-start.4 = (f32[256,3]{0,1:T(4,128)S(1)}, f32[256,3]{0,1:T(4,128)}, u32[]{:S(2)}) copy-start(f32[256,3]{0,1:T(4,128)} %param.24) | copy-start | bytes 9220
  7.9 40.6 %collective-permute-start = (f32[2,4,1,128]{3,1,2,0:T(4,128)S(1)}, f32[2,4,1,128]{3,1,2,0:T(4,128)S(1)}, u32[]{:S(2)}, u32[]{:S(2)}) collective-permute-start(f32[2,4,1,128]{3,1,2,0:T(4,128)S(1)} %pad_maximum_fusion.17), channel_id=1, source_target_pairs={{0,1},{1,2},{2,3},{3,4},{4,5},{5,6},{6,7},{8,9},{9,10},{10,11},{11... | collective-permute-start | bytes 12296 | tf_op jit(solution)/shard_map/ppermute | solution.py:30
  9.7 38.9 %collective-permute-start.1 = (f32[2,1,8,128]{3,1,2,0:T(1,128)S(1)}, f32[2,1,8,128]{3,1,2,0:T(1,128)S(1)}, u32[]{:S(2)}, u32[]{:S(2)}) collective-permute-start(f32[2,1,8,128]{3,1,2,0:T(1,128)S(1)} %pad_maximum_fusion.16), channel_id=1, source_target_pairs={{0,8},{8,16},{16,24},{24,32},{32,40},{40,48},{48,56},{56,64},{64,7... | collective-permute-start | bytes 24584 | tf_op jit(solution)/shard_map/ppermute | solution.py:30
  14.2 16.5 %collective-permute-start.10 = (f32[3,4,8,1]{3,2,1,0:T(8,128)S(1)}, f32[3,4,8,1]{3,2,1,0:T(8,128)S(1)}, u32[]{:S(2)}, u32[]{:S(2)}) collective-permute-start(f32[3,4,8,1]{3,2,1,0:T(8,128)S(1)} %get-tuple-element.101), channel_id=1, source_target_pairs={{0,128},{128,256},{256,384},{1,129},{129,257},{257,385},{2,130},{1... | collective-permute-start | bytes 1160 | tf_op jit(solution)/shard_map/ppermute | solution.py:18
  17.6 13.1 %collective-permute-start.11 = (f32[3,4,8,1]{3,2,1,0:T(8,128)S(1)}, f32[3,4,8,1]{3,2,1,0:T(8,128)S(1)}, u32[]{:S(2)}, u32[]{:S(2)}) collective-permute-start(f32[3,4,8,1]{3,2,1,0:T(8,128)S(1)} %get-tuple-element.102), channel_id=1, source_target_pairs={{128,0},{256,128},{384,256},{129,1},{257,129},{385,257},{130,2},{2... | collective-permute-start | bytes 1160 | tf_op jit(solution)/shard_map/ppermute | solution.py:20
  19.9 59.9 %collective-permute-start.2 = (f32[12,1,8,128]{3,1,2,0:T(1,128)S(1)}, f32[12,1,8,128]{3,1,2,0:T(1,128)S(1)}, u32[]{:S(2)}, u32[]{:S(2)}) collective-permute-start(f32[12,1,8,128]{3,1,2,0:T(1,128)S(1)} %get-tuple-element.69), channel_id=1, source_target_pairs={{0,8},{8,16},{16,24},{24,32},{32,40},{40,48},{48,56},{56,64},{64,7... | collective-permute-start | bytes 147464 | tf_op jit(solution)/shard_map/ppermute | solution.py:18
  30.8 6.6 %collective-permute-start.12 = (f32[3,1,8,34]{3,2,1,0:T(8,128)S(1)}, f32[3,1,8,34]{3,2,1,0:T(8,128)S(1)}, u32[]{:S(2)}, u32[]{:S(2)}) collective-permute-start(f32[3,1,8,34]{3,2,1,0:T(8,128)S(1)} %get-tuple-element.73), channel_id=1, source_target_pairs={{0,8},{8,16},{16,24},{24,32},{32,40},{40,48},{48,56},{56,64},{64,7... | collective-permute-start | bytes 9800 | tf_op jit(solution)/shard_map/ppermute | solution.py:18
  35.4 5.6 %collective-permute-start.13 = (f32[3,1,8,34]{3,2,1,0:T(8,128)S(1)}, f32[3,1,8,34]{3,2,1,0:T(8,128)S(1)}, u32[]{:S(2)}, u32[]{:S(2)}) collective-permute-start(f32[3,1,8,34]{3,2,1,0:T(8,128)S(1)} %get-tuple-element.74), channel_id=1, source_target_pairs={{8,0},{16,8},{24,16},{32,24},{40,32},{48,40},{56,48},{64,56},{72,6... | collective-permute-start | bytes 9800 | tf_op jit(solution)/shard_map/ppermute | solution.py:20
  41.2 3.8 %collective-permute-start.14 = (f32[3,6,1,34]{3,2,1,0:T(1,128)S(1)}, f32[3,6,1,34]{3,2,1,0:T(1,128)S(1)}, u32[]{:S(2)}, u32[]{:S(2)}) collective-permute-start(f32[3,6,1,34]{3,2,1,0:T(1,128)S(1)} %get-tuple-element.97), channel_id=1, source_target_pairs={{0,1},{1,2},{2,3},{3,4},{4,5},{5,6},{6,7},{8,9},{9,10},{10,11},{11... | collective-permute-start | bytes 7352 | tf_op jit(solution)/shard_map/ppermute | solution.py:18
  43.5 4.9 %collective-permute-start.15 = (f32[3,6,1,34]{3,2,1,0:T(1,128)S(1)}, f32[3,6,1,34]{3,2,1,0:T(1,128)S(1)}, u32[]{:S(2)}, u32[]{:S(2)}) collective-permute-start(f32[3,6,1,34]{3,2,1,0:T(1,128)S(1)} %get-tuple-element.98), channel_id=1, source_target_pairs={{1,0},{2,1},{3,2},{4,3},{5,4},{6,5},{7,6},{9,8},{10,9},{11,10},{12... | collective-permute-start | bytes 7352 | tf_op jit(solution)/shard_map/ppermute | solution.py:20
  44.9 4.3 %copy-start.1 = (f32[3,4,8,128]{3,2,1,0:T(8,128)S(1)}, f32[3,4,8,128]{3,2,1,0:T(8,128)}, u32[]{:S(2)}) copy-start(f32[3,4,8,128]{3,2,1,0:T(8,128)} %param.15) | copy-start | bytes 147460
  44.9 4.3 %copy-start.3 = (f32[3,4,8,128]{3,2,1,0:T(8,128)S(1)}, f32[3,4,8,128]{3,2,1,0:T(8,128)}, u32[]{:S(2)}) copy-start(f32[3,4,8,128]{3,2,1,0:T(8,128)} %param.16) | copy-start | bytes 147460
  45.0 34.9 %collective-permute-start.3 = (f32[12,1,8,128]{3,1,2,0:T(1,128)S(1)}, f32[12,1,8,128]{3,1,2,0:T(1,128)S(1)}, u32[]{:S(2)}, u32[]{:S(2)}) collective-permute-start(f32[12,1,8,128]{3,1,2,0:T(1,128)S(1)} %get-tuple-element.70), channel_id=1, source_target_pairs={{8,0},{16,8},{24,16},{32,24},{40,32},{48,40},{56,48},{64,56},{72,6... | collective-permute-start | bytes 147464 | tf_op jit(solution)/shard_map/ppermute | solution.py:20
  49.4 6.3 %collective-permute-start.16 = (f32[3,4,8,1]{3,2,1,0:T(8,128)S(1)}, f32[3,4,8,1]{3,2,1,0:T(8,128)S(1)}, u32[]{:S(2)}, u32[]{:S(2)}) collective-permute-start(f32[3,4,8,1]{3,2,1,0:T(8,128)S(1)} %get-tuple-element.99), channel_id=1, source_target_pairs={{0,128},{128,256},{256,384},{1,129},{129,257},{257,385},{2,130},{1... | collective-permute-start | bytes 1160 | tf_op jit(solution)/shard_map/ppermute | solution.py:18
  54.0 6.0 %collective-permute-start.17 = (f32[3,4,8,1]{3,2,1,0:T(8,128)S(1)}, f32[3,4,8,1]{3,2,1,0:T(8,128)S(1)}, u32[]{:S(2)}, u32[]{:S(2)}) collective-permute-start(f32[3,4,8,1]{3,2,1,0:T(8,128)S(1)} %get-tuple-element.100), channel_id=1, source_target_pairs={{128,0},{256,128},{384,256},{129,1},{257,129},{385,257},{130,2},{2... | collective-permute-start | bytes 1160 | tf_op jit(solution)/shard_map/ppermute | solution.py:20
  60.1 6.2 %collective-permute-start.18 = (f32[3,1,8,34]{3,2,1,0:T(8,128)S(1)}, f32[3,1,8,34]{3,2,1,0:T(8,128)S(1)}, u32[]{:S(2)}, u32[]{:S(2)}) collective-permute-start(f32[3,1,8,34]{3,2,1,0:T(8,128)S(1)} %get-tuple-element.71), channel_id=1, source_target_pairs={{0,8},{8,16},{16,24},{24,32},{32,40},{40,48},{48,56},{56,64},{64,7... | collective-permute-start | bytes 9800 | tf_op jit(solution)/shard_map/ppermute | solution.py:18
  62.6 5.7 %collective-permute-start.19 = (f32[3,1,8,34]{3,2,1,0:T(8,128)S(1)}, f32[3,1,8,34]{3,2,1,0:T(8,128)S(1)}, u32[]{:S(2)}, u32[]{:S(2)}) collective-permute-start(f32[3,1,8,34]{3,2,1,0:T(8,128)S(1)} %get-tuple-element.72), channel_id=1, source_target_pairs={{8,0},{16,8},{24,16},{32,24},{40,32},{48,40},{56,48},{64,56},{72,6... | collective-permute-start | bytes 9800 | tf_op jit(solution)/shard_map/ppermute | solution.py:20
  68.5 10.7 %collective-permute-start.20 = (f32[3,6,1,34]{3,2,1,0:T(1,128)S(1)}, f32[3,6,1,34]{3,2,1,0:T(1,128)S(1)}, u32[]{:S(2)}, u32[]{:S(2)}) collective-permute-start(f32[3,6,1,34]{3,2,1,0:T(1,128)S(1)} %get-tuple-element.91), channel_id=1, source_target_pairs={{0,1},{1,2},{2,3},{3,4},{4,5},{5,6},{6,7},{8,9},{9,10},{10,11},{11... | collective-permute-start | bytes 7352 | tf_op jit(solution)/shard_map/ppermute | solution.py:18
  70.5 8.6 %collective-permute-start.21 = (f32[3,6,1,34]{3,2,1,0:T(1,128)S(1)}, f32[3,6,1,34]{3,2,1,0:T(1,128)S(1)}, u32[]{:S(2)}, u32[]{:S(2)}) collective-permute-start(f32[3,6,1,34]{3,2,1,0:T(1,128)S(1)} %get-tuple-element.92), channel_id=1, source_target_pairs={{1,0},{2,1},{3,2},{4,3},{5,4},{6,5},{7,6},{9,8},{10,9},{11,10},{12... | collective-permute-start | bytes 7352 | tf_op jit(solution)/shard_map/ppermute | solution.py:20
  75.1 16.2 %all-to-all-start = ((f32[4,1,6144]{2,1,0:T(1,128)}), f32[4,1,6144]{2,1,0:T(1,128)S(1)}, u32[]{:S(2)}, u32[]{:S(2)}) async-start(f32[4,1,6144]{2,1,0:T(1,128)} %reshape.353), calls=%async_computation | async-start | bytes 196608 | tf_op jit(solution)/shard_map/all_to_all | solution.py:180
  79.9 19.8 %collective-permute-start.4 = (f32[12,6,1,128]{3,1,2,0:T(8,128)S(1)}, f32[12,6,1,128]{3,1,2,0:T(8,128)S(1)}, u32[]{:S(2)}, u32[]{:S(2)}) collective-permute-start(f32[12,6,1,128]{3,1,2,0:T(8,128)S(1)} %get-tuple-element.59), channel_id=1, source_target_pairs={{0,1},{1,2},{2,3},{3,4},{4,5},{5,6},{6,7},{8,9},{9,10},{10,11},{11... | collective-permute-start | bytes 110600 | tf_op jit(solution)/shard_map/ppermute | solution.py:18
  86.6 13.1 %collective-permute-start.5 = (f32[12,6,1,128]{3,1,2,0:T(8,128)S(1)}, f32[12,6,1,128]{3,1,2,0:T(8,128)S(1)}, u32[]{:S(2)}, u32[]{:S(2)}) collective-permute-start(f32[12,6,1,128]{3,1,2,0:T(8,128)S(1)} %get-tuple-element.60), channel_id=1, source_target_pairs={{1,0},{2,1},{3,2},{4,3},{5,4},{6,5},{7,6},{9,8},{10,9},{11,10},{12... | collective-permute-start | bytes 110600 | tf_op jit(solution)/shard_map/ppermute | solution.py:20
  91.3 28.7 %all-to-all-start.1 = ((f32[4,1,6144]{2,1,0:T(1,128)}), f32[4,1,6144]{2,1,0:T(1,128)S(1)}, u32[]{:S(2)}, u32[]{:S(2)}) async-start(f32[4,1,6144]{2,1,0:T(1,128)} %reshape.351), calls=%async_computation.1 | async-start | bytes 196608 | tf_op jit(solution)/shard_map/all_to_all | solution.py:180
  95.8 84.1 %reduce-scatter.4.cloned.1.call-start = ((), (), s32[]{:S(2)}) async-start(), calls=%async_computation.3 | async-start | bytes 81920
  101.4 0.9 copy-start
  101.4 1.0 copy-start.2
  102.6 7.9 %collective-permute-start.6 = (f32[12,1,8,128]{3,2,1,0:T(8,128)S(1)}, f32[12,1,8,128]{3,2,1,0:T(8,128)S(1)}, u32[]{:S(2)}, u32[]{:S(2)}) collective-permute-start(f32[12,1,8,128]{3,2,1,0:T(8,128)S(1)} %get-tuple-element.67), channel_id=1, source_target_pairs={{0,8},{8,16},{16,24},{24,32},{32,40},{40,48},{48,56},{56,64},{64,7... | collective-permute-start | bytes 147464 | tf_op jit(solution)/shard_map/ppermute | solution.py:18
  108.0 7.2 %collective-permute-start.7 = (f32[12,1,8,128]{3,2,1,0:T(8,128)S(1)}, f32[12,1,8,128]{3,2,1,0:T(8,128)S(1)}, u32[]{:S(2)}, u32[]{:S(2)}) collective-permute-start(f32[12,1,8,128]{3,2,1,0:T(8,128)S(1)} %get-tuple-element.68), channel_id=1, source_target_pairs={{8,0},{16,8},{24,16},{32,24},{40,32},{48,40},{56,48},{64,56},{72,6... | collective-permute-start | bytes 147464 | tf_op jit(solution)/shard_map/ppermute | solution.py:20
  115.2 8.2 %collective-permute-start.8 = (f32[12,6,1,128]{3,2,1,0:T(1,128)S(1)}, f32[12,6,1,128]{3,2,1,0:T(1,128)S(1)}, u32[]{:S(2)}, u32[]{:S(2)}) collective-permute-start(f32[12,6,1,128]{3,2,1,0:T(1,128)S(1)} %get-tuple-element.54), channel_id=1, source_target_pairs={{0,1},{1,2},{2,3},{3,4},{4,5},{5,6},{6,7},{8,9},{9,10},{10,11},{11... | collective-permute-start | bytes 110600 | tf_op jit(solution)/shard_map/ppermute | solution.py:18
  118.6 5.8 %collective-permute-start.9 = (f32[12,6,1,128]{3,2,1,0:T(1,128)S(1)}, f32[12,6,1,128]{3,2,1,0:T(1,128)S(1)}, u32[]{:S(2)}, u32[]{:S(2)}) collective-permute-start(f32[12,6,1,128]{3,2,1,0:T(1,128)S(1)} %get-tuple-element.55), channel_id=1, source_target_pairs={{1,0},{2,1},{3,2},{4,3},{5,4},{6,5},{7,6},{9,8},{10,9},{11,10},{12... | collective-permute-start | bytes 110600 | tf_op jit(solution)/shard_map/ppermute | solution.py:20
  128.0 0.7 copy-start.5
Sparse Core Ops, SparseCore 0:
  130.2 49.6 reduce-scatter.3
